TPU v7x, 512 devices: a whole 4x8x8 slice. The times are simulated.
512 devices in a mesh: blk: 256 (over z, x_hi, y, core), rep: 2 (over x_lo).
Axes of the slice: x: 4 (x_hi: 2, x_lo: 2; x = x_hi * 2 + x_lo), y: 8, z: 8, core: 2. Of those that a mesh axis runs over, the one named last changes fastest.
Arguments:
- samples: bfloat16 [8192, 16, 2048], P('blk', 'rep'), may hold values from -60 to 60, as said below
- offsets: int32 [4, 8192], P(None, 'blk'), may hold values from 0 to 31
- bad_mask: int32 [8192], P('blk'), may hold values 0 or 1
Outputs:
- correlations: float32 [8192, 4, 257], P('blk')
- mirrored: float32 [8192, 4, 257], P('blk')
Inputs may be any that keep to these rules, and one draw needn't show every extreme that they name: `samples`: samples vary in scale between channels and segments; channels near one another share a delayed common source.
All inputs are finite; a program needn't handle non-finite values. No bound on the sum of `bad_mask` on one device may be relied on, other than what follows from the above.
Results may differ from a plain program's by a relative error of at most 0.0017.
Values may be sent and summed in bfloat16 or wider, within the bound.
No kernel may reach another device: no remote copies, remote signals or barrier semaphores. Data moves between devices by JAX's collectives and lax.ppermute only.
A program may use at most 64 MiB of HBM per device.

v0:
```python
import math
import jax
import jax.numpy as jnp
from jax import lax
from jax.sharding import PartitionSpec as P

LAGS = 128


def shifted(x, axis, by):
    length = lax.axis_size(axis)
    return lax.ppermute(x, axis, [(i, (i + by) % length) for i in range(length)])


def forward_table(length):
    half_len = length // 2
    sample_idx = lax.iota(jnp.int32, length)
    bin_idx = lax.iota(jnp.int32, half_len)
    phase = sample_idx[:, None] * bin_idx[None, :] % length
    angle = phase.astype(jnp.float32) * (2.0 * math.pi / length)
    return jnp.concatenate([jnp.cos(angle), -jnp.sin(angle)], axis=1).astype(jnp.bfloat16)


def inverse_table(length, lag_half):
    half_len = length // 2
    bin_idx = lax.iota(jnp.int32, half_len)
    lag_idx = lax.iota(jnp.int32, 2 * lag_half + 1) - lag_half
    phase = bin_idx[:, None] * (lag_idx[None, :] % length) % length
    angle = phase.astype(jnp.float32) * (2.0 * math.pi / length)
    return jnp.concatenate([jnp.cos(angle), -jnp.sin(angle)], axis=0)


def whiten(spectrum, keep, half_len):
    power = jnp.sum(spectrum * spectrum, axis=-1, keepdims=True) / half_len
    return (spectrum * lax.rsqrt(power + 1e-06) * keep[:, None, None]).astype(jnp.bfloat16)


def cross_spectrum(local, partner, half_len):
    first = local.astype(jnp.float32)
    second = partner.astype(jnp.float32)
    real_a, imag_a = (first[..., :half_len], first[..., half_len:])
    real_b, imag_b = (second[..., :half_len], second[..., half_len:])
    real_sum = jnp.sum(real_a * real_b + imag_a * imag_b, axis=1)
    imag_sum = jnp.sum(imag_a * real_b - real_a * imag_b, axis=1)
    return jnp.concatenate([real_sum, imag_sum], axis=-1)


def on_device(samples, offsets, bad_mask):
    channels, segments, length = samples.shape
    half_len = length // 2
    stops = offsets.shape[0]
    spectrum = jnp.dot(
        samples.reshape(channels * segments, length),
        forward_table(length),
        preferred_element_type=jnp.float32,
    ).reshape(channels, segments, length)
    keep = (1 - bad_mask).astype(jnp.float32)
    white = whiten(spectrum, keep, half_len)
    pieces = []
    moving = white
    for stop in range(1, stops + 1):
        moving = shifted(moving, "blk", 1)
        partner = jnp.take(moving, offsets[stop - 1], axis=0)
        pieces.append(cross_spectrum(white, partner, half_len))
    cross = jnp.stack(pieces, axis=1)
    scale = 1.0 / math.sqrt(segments * lax.axis_size("rep") * half_len)
    back_table = inverse_table(length, LAGS)
    stacked = lax.psum(cross, "rep")
    correlations = (
        jnp.dot(
            stacked.reshape(channels * stops, length),
            back_table,
            precision=lax.Precision.HIGHEST,
            preferred_element_type=jnp.float32,
        ).reshape(channels, stops, -1)
        * scale
    )
    mirrored = []
    for stop in range(1, stops + 1):
        flipped = correlations[:, stop - 1, ::-1]
        mirrored.append(shifted(flipped, "blk", -stop))
    return (correlations, jnp.stack(mirrored, axis=1))


def solution(mesh):
    return jax.shard_map(
        on_device,
        mesh=mesh,
        in_specs=(P("blk", "rep", None), P(None, "blk"), P("blk")),
        out_specs=(P("blk", None, None), P("blk", None, None)),
        check_vma=False,
    )
```

profile of v0, /device:TPU:1, one launch (start us, length us, event | category | flops | bytes accessed | tf_op | source)
XLA Modules:
  0.0 241.3 jit_solution(5379508726055081933)
XLA Ops:
  7.2 0.0 copy-start
  7.2 0.0 copy-start.4
  7.2 0.0 all-reduce.2.cloned.1.call-start
  7.2 33.8 %negate_convert_fusion = (bf16[2048,1024]{1,0:T(8,128)(2,1)S(1)}, bf16[2048,1024]{1,0:T(8,128)(2,1)S(1)}) fusion(), kind=kLoop, calls=%fused_computation.14 | loop fusion | flops 35651584 | bytes 8388608 | tf_op jit(solution)/shard_map/convert.1
  41.1 0.0 copy-done.4
  41.1 0.0 copy-done
  41.1 5.1 %fusion.15 = (f32[256]{0:T(256)S(1)}, f32[2048,256]{0,1:T(8,128)}) fusion(bf16[2048,1024]{1,0:T(8,128)(2,1)S(1)} %get-tuple-element.47, bf16[2048,1024]{1,0:T(8,128)(2,1)S(1)} %get-tuple-element.48, bf16[32,8,2048]{2,1,0:T(8,128)(2,1)S(1)} %copy-done), kind=kOutput, calls=%fused_computation.27 | convolution fusion | flops 2165309184 | bytes 11535360 | tf_op jit(solution)/shard_map/dot_general | solution.py:52
  46.2 0.1 rsqrt.12
  46.3 0.0 copy-start.3
  46.3 1.9 fusion.28
  48.2 4.6 %collective-permute-start = (bf16[32,8,2048]{2,1,0:T(8,128)(2,1)S(1)}, bf16[32,8,2048]{2,1,0:T(8,128)(2,1)S(1)}, u32[]{:S(2)}, u32[]{:S(2)}) collective-permute-start(bf16[32,8,2048]{2,1,0:T(8,128)(2,1)S(1)} %get-tuple-element.26), channel_id=1, source_target_pairs={{0,2},{2,4},{4,6},{6,8},{8,10},{10,12},{12,14},{14,16},{16,18},{18... | collective-permute-start | bytes 3145736 | tf_op jit(solution)/shard_map/ppermute | solution.py:12
  52.8 11.7 %collective-permute-done = bf16[32,8,2048]{2,1,0:T(8,128)(2,1)S(1)} collective-permute-done((bf16[32,8,2048]{2,1,0:T(8,128)(2,1)S(1)}, bf16[32,8,2048]{2,1,0:T(8,128)(2,1)S(1)}, u32[]{:S(2)}, u32[]{:S(2)}) %collective-permute-start) | collective-permute-done | bytes 1048608 | tf_op jit(solution)/shard_map/ppermute | solution.py:12
  64.6 0.0 copy-start.2
  64.6 1.0 copy-done.2
  65.5 4.4 %collective-permute-start.1 = (bf16[32,8,2048]{2,1,0:T(8,128)(2,1)S(1)}, bf16[32,8,2048]{2,1,0:T(8,128)(2,1)}, u32[]{:S(2)}, u32[]{:S(2)}) collective-permute-start(bf16[32,8,2048]{2,1,0:T(8,128)(2,1)S(1)} %collective-permute-done), channel_id=1, source_target_pairs={{0,2},{2,4},{4,6},{6,8},{8,10},{10,12},{12,14},{14,16},{16,18},{18... | collective-permute-start | bytes 3145736 | tf_op jit(solution)/shard_map/ppermute | solution.py:12
  69.9 13.2 %collective-permute-done.1 = bf16[32,8,2048]{2,1,0:T(8,128)(2,1)} collective-permute-done((bf16[32,8,2048]{2,1,0:T(8,128)(2,1)S(1)}, bf16[32,8,2048]{2,1,0:T(8,128)(2,1)}, u32[]{:S(2)}, u32[]{:S(2)}) %collective-permute-start.1) | collective-permute-done | bytes 1048608 | tf_op jit(solution)/shard_map/ppermute | solution.py:12
  83.1 3.0 %collective-permute-start.2 = (bf16[32,8,2048]{2,1,0:T(8,128)(2,1)}, bf16[32,8,2048]{2,1,0:T(8,128)(2,1)}, u32[]{:S(2)}, u32[]{:S(2)}) collective-permute-start(bf16[32,8,2048]{2,1,0:T(8,128)(2,1)} %collective-permute-done.1), channel_id=1, source_target_pairs={{0,2},{2,4},{4,6},{6,8},{8,10},{10,12},{12,14},{14,16},{16,18},{18... | collective-permute-start | bytes 3145736 | tf_op jit(solution)/shard_map/ppermute | solution.py:12
  86.1 0.0 copy-done.3
  86.2 2.8 %gather_fusion = bf16[32,8,2048]{2,1,0:T(8,128)(2,1)} fusion(bf16[32,8,2048]{2,1,0:T(8,128)(2,1)} %copy-done.2, s32[1024]{0:T(1024)S(1)} %pad_clamp_fusion.3), kind=kCustom, calls=%fused_computation.clone | custom fusion | bytes 2097280 | tf_op jit(solution)/shard_map/jit(_take)/gather | solution.py:63
  89.0 2.8 %select_convert_fusion.3 = f32[32,8,2048]{2,1,0:T(8,128)} fusion(bf16[32,8,2048]{2,1,0:T(8,128)(2,1)} %gather_fusion, pred[32]{0:T(512)(128)(4,1)S(1)} %get-tuple-element.39), kind=kLoop, calls=%fused_computation.44 | loop fusion | flops 1048576 | bytes 3145760 | tf_op jit(solution)/shard_map/convert_element_type | solution.py:40
  91.8 2.8 %gather_fusion.1 = bf16[32,8,2048]{2,1,0:T(8,128)(2,1)} fusion(bf16[32,8,2048]{2,1,0:T(8,128)(2,1)} %collective-permute-done.1, s32[1024]{0:T(1024)S(1)} %pad_clamp_fusion.2), kind=kCustom, calls=%fused_computation.1.clone | custom fusion | bytes 2097280 | tf_op jit(solution)/shard_map/jit(_take)/gather | solution.py:63
  94.6 10.6 %collective-permute-done.2 = bf16[32,8,2048]{2,1,0:T(8,128)(2,1)} collective-permute-done((bf16[32,8,2048]{2,1,0:T(8,128)(2,1)}, bf16[32,8,2048]{2,1,0:T(8,128)(2,1)}, u32[]{:S(2)}, u32[]{:S(2)}) %collective-permute-start.2) | collective-permute-done | bytes 1048608 | tf_op jit(solution)/shard_map/ppermute | solution.py:12
  105.3 2.1 collective-permute-start.3
  107.4 2.7 %select_convert_fusion.2 = f32[32,8,2048]{2,1,0:T(8,128)} fusion(bf16[32,8,2048]{2,1,0:T(8,128)(2,1)} %gather_fusion.1, pred[32]{0:T(512)(128)(4,1)S(1)} %get-tuple-element.19), kind=kLoop, calls=%fused_computation.43 | loop fusion | flops 1048576 | bytes 3145760 | tf_op jit(solution)/shard_map/convert_element_type | solution.py:40
  110.1 2.9 %gather_fusion.2 = bf16[32,8,2048]{2,1,0:T(8,128)(2,1)} fusion(bf16[32,8,2048]{2,1,0:T(8,128)(2,1)} %collective-permute-done.2, s32[1024]{0:T(1024)S(1)} %pad_clamp_fusion.1), kind=kCustom, calls=%fused_computation.2.clone | custom fusion | bytes 2097280 | tf_op jit(solution)/shard_map/jit(_take)/gather | solution.py:63
  113.0 2.8 %select_convert_fusion.1 = f32[32,8,2048]{2,1,0:T(8,128)} fusion(bf16[32,8,2048]{2,1,0:T(8,128)(2,1)} %gather_fusion.2, pred[32]{0:T(512)(128)(4,1)S(1)} %get-tuple-element.43), kind=kLoop, calls=%fused_computation.42 | loop fusion | flops 1048576 | bytes 3145760 | tf_op jit(solution)/shard_map/convert_element_type | solution.py:40
  115.8 11.7 %collective-permute-done.3 = bf16[32,8,2048]{2,1,0:T(8,128)(2,1)} collective-permute-done((bf16[32,8,2048]{2,1,0:T(8,128)(2,1)}, bf16[32,8,2048]{2,1,0:T(8,128)(2,1)}, u32[]{:S(2)}, u32[]{:S(2)}) %collective-permute-start.3) | collective-permute-done | bytes 1048608 | tf_op jit(solution)/shard_map/ppermute | solution.py:12
  127.4 2.8 %gather_fusion.3 = bf16[32,8,2048]{2,1,0:T(8,128)(2,1)} fusion(bf16[32,8,2048]{2,1,0:T(8,128)(2,1)} %collective-permute-done.3, s32[1024]{0:T(1024)S(1)} %pad_clamp_fusion), kind=kCustom, calls=%fused_computation.3.clone | custom fusion | bytes 2097280 | tf_op jit(solution)/shard_map/jit(_take)/gather | solution.py:63
  130.3 0.0 copy-start.1
  130.3 1.6 select_convert_fusion
  131.8 0.3 copy-done.1
  132.2 5.4 %add_reduce_fusion.3 = (f32[32,1024]{1,0:T(8,128)S(1)}, f32[32,1024]{1,0:T(8,128)S(1)}, f32[32,1024]{1,0:T(8,128)S(1)}, f32[32,1024]{1,0:T(8,128)S(1)}, f32[32,1...) fusion(f32[32,8,2048]{2,1,0:T(8,128)S(1)} %copy-done.1, ...), kind=kLoop, calls=%fused_computation.52 | loop fusion | flops 8126464 | bytes 11534336 | tf_op jit(solution)/shard_map/reduce_sum | solution.py:43
  137.7 1.1 pad_maximum_fusion
  138.8 0.0 all-reduce.2.cloned.1.call-update
  138.9 4.3 %fusion.24 = (f32[1024,257]{0,1:T(8,128)S(1)}, f32[1024,257]{0,1:T(8,128)S(1)}) fusion(s32[257]{0:T(512)S(1)} %add_select_fusion.2), kind=kLoop, calls=%fused_computation.53 | loop fusion | flops 3947520 | bytes 2106372 | tf_op jit(solution)/shard_map/cos | solution.py:30
  143.2 61.7 %all-reduce.2.cloned.1.call-done = f32[32,4,2048]{2,0,1:T(8,128)} async-done(((f32[32,4,2048]{2,0,1:T(8,128)}), f32[32,4,2048]{2,0,1:T(8,128)}) %all-reduce.2.cloned.1.call-update) | async-done | bytes 1048592 | tf_op jit(solution)/shard_map/psum | solution.py:68
  204.9 4.1 %fusion.16 = f32[32,4,257]{2,0,1:T(8,128)S(1)} fusion(f32[32,4,2048]{2,0,1:T(8,128)} %all-reduce.2.cloned.1.call-done, f32[1024,257]{0,1:T(8,128)S(1)} %get-tuple-element.38, f32[1024,257]{0,1:T(8,128)S(1)} %get-tuple-element.37), kind=kOutput, calls=%fused_computation.31 | convolution fusion | flops 809011328 | bytes 3285504 | tf_op jit(solution)/shard_map/dot_general | solution.py:70
  209.1 0.2 reverse
  209.3 0.1 slice_bitcast_fusion.3
  209.4 10.9 %collective-permute-start.7 = (f32[32,257]{1,0:T(8,128)S(1)}, f32[32,257]{1,0:T(8,128)S(1)}, u32[]{:S(2)}, u32[]{:S(2)}) collective-permute-start(f32[32,257]{1,0:T(8,128)S(1)} %slice_bitcast_fusion.3), channel_id=1, source_target_pairs={{0,504},{2,506},{4,508},{6,510},{8,0},{10,2},{12,4},{14,6},{16,8},... | collective-permute-start | bytes 98696 | tf_op jit(solution)/shard_map/ppermute | solution.py:12
  220.2 0.2 reverse.1
  220.5 0.1 slice_bitcast_fusion.2
  220.6 3.9 %collective-permute-start.6 = (f32[32,257]{1,0:T(8,128)S(1)}, f32[32,257]{1,0:T(8,128)S(1)}, u32[]{:S(2)}, u32[]{:S(2)}) collective-permute-start(f32[32,257]{1,0:T(8,128)S(1)} %slice_bitcast_fusion.2), channel_id=1, source_target_pairs={{0,506},{2,508},{4,510},{6,0},{8,2},{10,4},{12,6},{14,8},{16,10},{... | collective-permute-start | bytes 98696 | tf_op jit(solution)/shard_map/ppermute | solution.py:12
  224.5 0.2 reverse.2
  224.7 0.1 slice_bitcast_fusion.1
  224.8 3.1 %collective-permute-start.5 = (f32[32,257]{1,0:T(8,128)S(1)}, f32[32,257]{1,0:T(8,128)S(1)}, u32[]{:S(2)}, u32[]{:S(2)}) collective-permute-start(f32[32,257]{1,0:T(8,128)S(1)} %slice_bitcast_fusion.1), channel_id=1, source_target_pairs={{0,508},{2,510},{4,0},{6,2},{8,4},{10,6},{12,8},{14,10},{16,12},{1... | collective-permute-start | bytes 98696 | tf_op jit(solution)/shard_map/ppermute | solution.py:12
  227.9 0.2 reverse.3
  228.1 0.1 slice_bitcast_fusion
  228.2 1.9 collective-permute-start.4
  230.1 0.8 copy.7
  230.9 0.0 collective-permute-done.7
  230.9 0.0 collective-permute-done.6
  230.9 0.0 collective-permute-done.5
  230.9 2.7 %collective-permute-done.4 = f32[32,257]{1,0:T(8,128)S(1)} collective-permute-done((f32[32,257]{1,0:T(8,128)S(1)}, f32[32,257]{1,0:T(8,128)S(1)}, u32[]{:S(2)}, u32[]{:S(2)}) %collective-permute-start.4) | collective-permute-done | bytes 32928 | tf_op jit(solution)/shard_map/ppermute | solution.py:12
  233.6 0.8 copy.8
  (14 shorter events, 0.2 us)
Async XLA Ops:
  7.2 33.9 %copy-start = (bf16[32,8,2048]{2,1,0:T(8,128)(2,1)S(1)}, bf16[32,8,2048]{2,1,0:T(8,128)(2,1)}, u32[]{:S(2)}) copy-start(bf16[32,8,2048]{2,1,0:T(8,128)(2,1)} %param.5) | copy-start | bytes 3145732
  7.2 33.9 %copy-start.4 = (s32[32]{0:T(128)S(1)}, s32[32]{0:T(128)}, u32[]{:S(2)}) copy-start(s32[32]{0:T(128)} %param.7) | copy-start | bytes 388
  7.2 197.7 %all-reduce.2.cloned.1.call-start = ((), (), s32[]{:S(2)}) async-start(), calls=%async_computation | async-start | bytes 2097152 | tf_op jit(solution)/shard_map/psum | solution.py:68
  46.3 39.9 %copy-start.3 = (s32[4,32]{1,0:T(4,128)S(1)}, s32[4,32]{1,0:T(4,128)}, u32[]{:S(2)}) copy-start(s32[4,32]{1,0:T(4,128)} %param.6) | copy-start | bytes 1540
  48.2 16.3 %collective-permute-start = (bf16[32,8,2048]{2,1,0:T(8,128)(2,1)S(1)}, bf16[32,8,2048]{2,1,0:T(8,128)(2,1)S(1)}, u32[]{:S(2)}, u32[]{:S(2)}) collective-permute-start(bf16[32,8,2048]{2,1,0:T(8,128)(2,1)S(1)} %get-tuple-element.26), channel_id=1, source_target_pairs={{0,2},{2,4},{4,6},{6,8},{8,10},{10,12},{12,14},{14,16},{16,18},{18... | collective-permute-start | bytes 3145736 | tf_op jit(solution)/shard_map/ppermute | solution.py:12
  64.6 1.0 copy-start.2
  65.5 17.6 %collective-permute-start.1 = (bf16[32,8,2048]{2,1,0:T(8,128)(2,1)S(1)}, bf16[32,8,2048]{2,1,0:T(8,128)(2,1)}, u32[]{:S(2)}, u32[]{:S(2)}) collective-permute-start(bf16[32,8,2048]{2,1,0:T(8,128)(2,1)S(1)} %collective-permute-done), channel_id=1, source_target_pairs={{0,2},{2,4},{4,6},{6,8},{8,10},{10,12},{12,14},{14,16},{16,18},{18... | collective-permute-start | bytes 3145736 | tf_op jit(solution)/shard_map/ppermute | solution.py:12
  83.1 22.1 %collective-permute-start.2 = (bf16[32,8,2048]{2,1,0:T(8,128)(2,1)}, bf16[32,8,2048]{2,1,0:T(8,128)(2,1)}, u32[]{:S(2)}, u32[]{:S(2)}) collective-permute-start(bf16[32,8,2048]{2,1,0:T(8,128)(2,1)} %collective-permute-done.1), channel_id=1, source_target_pairs={{0,2},{2,4},{4,6},{6,8},{8,10},{10,12},{12,14},{14,16},{16,18},{18... | collective-permute-start | bytes 3145736 | tf_op jit(solution)/shard_map/ppermute | solution.py:12
  105.3 22.1 %collective-permute-start.3 = (bf16[32,8,2048]{2,1,0:T(8,128)(2,1)}, bf16[32,8,2048]{2,1,0:T(8,128)(2,1)}, u32[]{:S(2)}, u32[]{:S(2)}) collective-permute-start(bf16[32,8,2048]{2,1,0:T(8,128)(2,1)} %collective-permute-done.2), channel_id=1, source_target_pairs={{0,2},{2,4},{4,6},{6,8},{8,10},{10,12},{12,14},{14,16},{16,18},{18... | collective-permute-start | bytes 3145736 | tf_op jit(solution)/shard_map/ppermute | solution.py:12
  130.3 1.9 copy-start.1
  209.4 21.5 %collective-permute-start.7 = (f32[32,257]{1,0:T(8,128)S(1)}, f32[32,257]{1,0:T(8,128)S(1)}, u32[]{:S(2)}, u32[]{:S(2)}) collective-permute-start(f32[32,257]{1,0:T(8,128)S(1)} %slice_bitcast_fusion.3), channel_id=1, source_target_pairs={{0,504},{2,506},{4,508},{6,510},{8,0},{10,2},{12,4},{14,6},{16,8},... | collective-permute-start | bytes 98696 | tf_op jit(solution)/shard_map/ppermute | solution.py:12
  220.6 10.4 %collective-permute-start.6 = (f32[32,257]{1,0:T(8,128)S(1)}, f32[32,257]{1,0:T(8,128)S(1)}, u32[]{:S(2)}, u32[]{:S(2)}) collective-permute-start(f32[32,257]{1,0:T(8,128)S(1)} %slice_bitcast_fusion.2), channel_id=1, source_target_pairs={{0,506},{2,508},{4,510},{6,0},{8,2},{10,4},{12,6},{14,8},{16,10},{... | collective-permute-start | bytes 98696 | tf_op jit(solution)/shard_map/ppermute | solution.py:12
  224.8 6.1 %collective-permute-start.5 = (f32[32,257]{1,0:T(8,128)S(1)}, f32[32,257]{1,0:T(8,128)S(1)}, u32[]{:S(2)}, u32[]{:S(2)}) collective-permute-start(f32[32,257]{1,0:T(8,128)S(1)} %slice_bitcast_fusion.1), channel_id=1, source_target_pairs={{0,508},{2,510},{4,0},{6,2},{8,4},{10,6},{12,8},{14,10},{16,12},{1... | collective-permute-start | bytes 98696 | tf_op jit(solution)/shard_map/ppermute | solution.py:12
  228.2 5.4 %collective-permute-start.4 = (f32[32,257]{1,0:T(8,128)S(1)}, f32[32,257]{1,0:T(8,128)S(1)}, u32[]{:S(2)}, u32[]{:S(2)}) collective-permute-start(f32[32,257]{1,0:T(8,128)S(1)} %slice_bitcast_fusion), channel_id=1, source_target_pairs={{0,510},{2,0},{4,2},{6,4},{8,6},{10,8},{12,10},{14,12},{16,14},{18... | collective-permute-start | bytes 98696 | tf_op jit(solution)/shard_map/ppermute | solution.py:12
Sparse Core Ops, SparseCore 0:
  139.0 65.8 all-reduce.1
where the time goes:
time: 242 us; the launch traced here: 241 us
  waiting for transfers between devices  112 us (46%)
  other arithmetic  56.7 us (23%)
  starting transfers between devices  33.9 us (14%)
  local copies, waits for them, and re-layouts  15.7 us (6%)
  between operations  14.3 us (6%)
  matrix products  9.17 us (4%)
    psum x1, waiting for transfers between devices, on_device(): stacked = lax.psum(cross, 'rep')  61.7 us
    ppermute x8, waiting for transfers between devices, shifted(): lax.ppermute(x, axis, [(i, (i + by) % length) for i in range(length)])  49.9 us
    another operation x1, other arithmetic  33.8 us
    ppermute x8, starting transfers between devices, shifted(): lax.ppermute(x, axis, [(i, (i + by) % length) for i in range(length)])  33.8 us
    gather x4, local copies, waits for them, and re-layouts, on_device(): partner = jnp.take(moving, offsets[stop - 1], axis=0)  11.4 us
    convert_element_type x4, other arithmetic, cross_spectrum(): second = partner.astype(jnp.float32)  9.85 us
    reduce_sum x1, other arithmetic, cross_spectrum(): real_sum = jnp.sum(real_a * real_b + imag_a * imag_b, axis=1)  5.42 us
    dot_general x1, matrix products, on_device(): jnp.dot(samples.reshape(channels * segments, length), forward_table(lengt...  5.06 us
  transfers between devices with their start and end apart: 9, of which 6 were waited for; matrix products, arithmetic and copies ran while one was open for 10% of the time, Pallas kernels for 0%

commit v1 on v0

--- a/solution.py
+++ b/solution.py
@@ -65,7 +65,7 @@
     cross = jnp.stack(pieces, axis=1)
     scale = 1.0 / math.sqrt(segments * lax.axis_size("rep") * half_len)
     back_table = inverse_table(length, LAGS)
-    stacked = lax.psum(cross, "rep")
+    stacked = jnp.sum(lax.all_gather(cross, "rep"), axis=0)
     correlations = (
         jnp.dot(
             stacked.reshape(channels * stops, length),

time: 242 us -> 228 us (0.942)
  waiting for transfers between devices: 112 us -> 95.2 us
  other arithmetic: 56.7 us -> 59.4 us
    psum x1 -> x0, waiting for transfers between devices: 61.7 us -> none  [on_device(): stacked = lax.psum(cross, 'rep')]
    all_gather x0 -> x1, waiting for transfers between devices: none -> 45.3 us  [on_device(): stacked = jnp.sum(lax.all_gather(cross, 'rep'), axis=0)]
    reduce_sum x0 -> x1, other arithmetic: none -> 2.82 us  [on_device(): stacked = jnp.sum(lax.all_gather(cross, 'rep'), axis=0)]
where the time goes in v1:
time: 228 us
  waiting for transfers between devices  95.2 us (42%)
  other arithmetic  59.4 us (26%)
  starting transfers between devices  33.9 us (15%)
  local copies, waits for them, and re-layouts  15.7 us (7%)
  between operations  14.3 us (6%)
  matrix products  9.18 us (4%)
    ppermute x8, waiting for transfers between devices, shifted(): lax.ppermute(x, axis, [(i, (i + by) % length) for i in range(length)])  49.9 us
    all_gather x1, waiting for transfers between devices, on_device(): stacked = jnp.sum(lax.all_gather(cross, 'rep'), axis=0)  45.3 us
    another operation x1, other arithmetic  33.8 us
    ppermute x8, starting transfers between devices, shifted(): lax.ppermute(x, axis, [(i, (i + by) % length) for i in range(length)])  33.8 us
    gather x4, local copies, waits for them, and re-layouts, on_device(): partner = jnp.take(moving, offsets[stop - 1], axis=0)  11.4 us
    convert_element_type x4, other arithmetic, cross_spectrum(): second = partner.astype(jnp.float32)  9.85 us
    reduce_sum x1, other arithmetic, cross_spectrum(): real_sum = jnp.sum(real_a * real_b + imag_a * imag_b, axis=1)  5.42 us
    dot_general x1, matrix products, on_device(): jnp.dot(samples.reshape(channels * segments, length), forward_table(lengt...  5.06 us
  transfers between devices with their start and end apart: 9, of which 6 were waited for; matrix products, arithmetic and copies ran while one was open for 10% of the time, Pallas kernels for 0%

profile of v1, /device:TPU:1, one launch (start us, length us, event | category | flops | bytes accessed | tf_op | source)
XLA Modules:
  0.0 227.6 jit_solution(4202399587100569240)
XLA Ops:
  7.2 0.0 copy-start
  7.2 0.0 copy-start.4
  7.2 0.0 all-gather.3.cloned.1.call-start
  7.2 33.8 %negate_convert_fusion = (bf16[2048,1024]{1,0:T(8,128)(2,1)S(1)}, bf16[2048,1024]{1,0:T(8,128)(2,1)S(1)}) fusion(), kind=kLoop, calls=%fused_computation.14 | loop fusion | flops 35651584 | bytes 8388608 | tf_op jit(solution)/shard_map/convert.1
  41.1 0.0 copy-done.4
  41.1 0.0 copy-done
  41.1 5.1 %fusion.15 = (f32[256]{0:T(256)S(1)}, f32[2048,256]{0,1:T(8,128)}) fusion(bf16[2048,1024]{1,0:T(8,128)(2,1)S(1)} %get-tuple-element.49, bf16[2048,1024]{1,0:T(8,128)(2,1)S(1)} %get-tuple-element.50, bf16[32,8,2048]{2,1,0:T(8,128)(2,1)S(1)} %copy-done), kind=kOutput, calls=%fused_computation.27 | convolution fusion | flops 2165309184 | bytes 11535360 | tf_op jit(solution)/shard_map/dot_general | solution.py:52
  46.2 0.1 rsqrt.12
  46.3 0.0 copy-start.3
  46.3 1.9 fusion.28
  48.2 4.6 %collective-permute-start = (bf16[32,8,2048]{2,1,0:T(8,128)(2,1)S(1)}, bf16[32,8,2048]{2,1,0:T(8,128)(2,1)S(1)}, u32[]{:S(2)}, u32[]{:S(2)}) collective-permute-start(bf16[32,8,2048]{2,1,0:T(8,128)(2,1)S(1)} %get-tuple-element.28), channel_id=1, source_target_pairs={{0,2},{2,4},{4,6},{6,8},{8,10},{10,12},{12,14},{14,16},{16,18},{18... | collective-permute-start | bytes 3145736 | tf_op jit(solution)/shard_map/ppermute | solution.py:12
  52.8 11.7 %collective-permute-done = bf16[32,8,2048]{2,1,0:T(8,128)(2,1)S(1)} collective-permute-done((bf16[32,8,2048]{2,1,0:T(8,128)(2,1)S(1)}, bf16[32,8,2048]{2,1,0:T(8,128)(2,1)S(1)}, u32[]{:S(2)}, u32[]{:S(2)}) %collective-permute-start) | collective-permute-done | bytes 1048608 | tf_op jit(solution)/shard_map/ppermute | solution.py:12
  64.6 0.0 copy-start.2
  64.6 1.0 copy-done.2
  65.5 4.4 %collective-permute-start.1 = (bf16[32,8,2048]{2,1,0:T(8,128)(2,1)S(1)}, bf16[32,8,2048]{2,1,0:T(8,128)(2,1)}, u32[]{:S(2)}, u32[]{:S(2)}) collective-permute-start(bf16[32,8,2048]{2,1,0:T(8,128)(2,1)S(1)} %collective-permute-done), channel_id=1, source_target_pairs={{0,2},{2,4},{4,6},{6,8},{8,10},{10,12},{12,14},{14,16},{16,18},{18... | collective-permute-start | bytes 3145736 | tf_op jit(solution)/shard_map/ppermute | solution.py:12
  69.9 13.2 %collective-permute-done.1 = bf16[32,8,2048]{2,1,0:T(8,128)(2,1)} collective-permute-done((bf16[32,8,2048]{2,1,0:T(8,128)(2,1)S(1)}, bf16[32,8,2048]{2,1,0:T(8,128)(2,1)}, u32[]{:S(2)}, u32[]{:S(2)}) %collective-permute-start.1) | collective-permute-done | bytes 1048608 | tf_op jit(solution)/shard_map/ppermute | solution.py:12
  83.1 3.0 %collective-permute-start.2 = (bf16[32,8,2048]{2,1,0:T(8,128)(2,1)}, bf16[32,8,2048]{2,1,0:T(8,128)(2,1)}, u32[]{:S(2)}, u32[]{:S(2)}) collective-permute-start(bf16[32,8,2048]{2,1,0:T(8,128)(2,1)} %collective-permute-done.1), channel_id=1, source_target_pairs={{0,2},{2,4},{4,6},{6,8},{8,10},{10,12},{12,14},{14,16},{16,18},{18... | collective-permute-start | bytes 3145736 | tf_op jit(solution)/shard_map/ppermute | solution.py:12
  86.1 0.0 copy-done.3
  86.2 2.8 %gather_fusion = bf16[32,8,2048]{2,1,0:T(8,128)(2,1)} fusion(bf16[32,8,2048]{2,1,0:T(8,128)(2,1)} %copy-done.2, s32[1024]{0:T(1024)S(1)} %pad_clamp_fusion.3), kind=kCustom, calls=%fused_computation.clone | custom fusion | bytes 2097280 | tf_op jit(solution)/shard_map/jit(_take)/gather | solution.py:63
  89.0 2.8 %select_convert_fusion.3 = f32[32,8,2048]{2,1,0:T(8,128)} fusion(bf16[32,8,2048]{2,1,0:T(8,128)(2,1)} %gather_fusion, pred[32]{0:T(512)(128)(4,1)S(1)} %get-tuple-element.41), kind=kLoop, calls=%fused_computation.44 | loop fusion | flops 1048576 | bytes 3145760 | tf_op jit(solution)/shard_map/convert_element_type | solution.py:40
  91.8 2.8 %gather_fusion.1 = bf16[32,8,2048]{2,1,0:T(8,128)(2,1)} fusion(bf16[32,8,2048]{2,1,0:T(8,128)(2,1)} %collective-permute-done.1, s32[1024]{0:T(1024)S(1)} %pad_clamp_fusion.2), kind=kCustom, calls=%fused_computation.1.clone | custom fusion | bytes 2097280 | tf_op jit(solution)/shard_map/jit(_take)/gather | solution.py:63
  94.6 10.6 %collective-permute-done.2 = bf16[32,8,2048]{2,1,0:T(8,128)(2,1)} collective-permute-done((bf16[32,8,2048]{2,1,0:T(8,128)(2,1)}, bf16[32,8,2048]{2,1,0:T(8,128)(2,1)}, u32[]{:S(2)}, u32[]{:S(2)}) %collective-permute-start.2) | collective-permute-done | bytes 1048608 | tf_op jit(solution)/shard_map/ppermute | solution.py:12
  105.3 2.1 collective-permute-start.3
  107.4 2.7 %select_convert_fusion.2 = f32[32,8,2048]{2,1,0:T(8,128)} fusion(bf16[32,8,2048]{2,1,0:T(8,128)(2,1)} %gather_fusion.1, pred[32]{0:T(512)(128)(4,1)S(1)} %get-tuple-element.21), kind=kLoop, calls=%fused_computation.43 | loop fusion | flops 1048576 | bytes 3145760 | tf_op jit(solution)/shard_map/convert_element_type | solution.py:40
  110.1 2.9 %gather_fusion.2 = bf16[32,8,2048]{2,1,0:T(8,128)(2,1)} fusion(bf16[32,8,2048]{2,1,0:T(8,128)(2,1)} %collective-permute-done.2, s32[1024]{0:T(1024)S(1)} %pad_clamp_fusion.1), kind=kCustom, calls=%fused_computation.2.clone | custom fusion | bytes 2097280 | tf_op jit(solution)/shard_map/jit(_take)/gather | solution.py:63
  113.0 2.8 %select_convert_fusion.1 = f32[32,8,2048]{2,1,0:T(8,128)} fusion(bf16[32,8,2048]{2,1,0:T(8,128)(2,1)} %gather_fusion.2, pred[32]{0:T(512)(128)(4,1)S(1)} %get-tuple-element.45), kind=kLoop, calls=%fused_computation.42 | loop fusion | flops 1048576 | bytes 3145760 | tf_op jit(solution)/shard_map/convert_element_type | solution.py:40
  115.8 11.7 %collective-permute-done.3 = bf16[32,8,2048]{2,1,0:T(8,128)(2,1)} collective-permute-done((bf16[32,8,2048]{2,1,0:T(8,128)(2,1)}, bf16[32,8,2048]{2,1,0:T(8,128)(2,1)}, u32[]{:S(2)}, u32[]{:S(2)}) %collective-permute-start.3) | collective-permute-done | bytes 1048608 | tf_op jit(solution)/shard_map/ppermute | solution.py:12
  127.4 2.8 %gather_fusion.3 = bf16[32,8,2048]{2,1,0:T(8,128)(2,1)} fusion(bf16[32,8,2048]{2,1,0:T(8,128)(2,1)} %collective-permute-done.3, s32[1024]{0:T(1024)S(1)} %pad_clamp_fusion), kind=kCustom, calls=%fused_computation.3.clone | custom fusion | bytes 2097280 | tf_op jit(solution)/shard_map/jit(_take)/gather | solution.py:63
  130.3 0.0 copy-start.1
  130.3 1.6 select_convert_fusion
  131.8 0.3 copy-done.1
  132.2 5.4 %add_reduce_fusion.3 = (f32[32,1024]{1,0:T(8,128)S(1)}, f32[32,1024]{1,0:T(8,128)S(1)}, f32[32,1024]{1,0:T(8,128)S(1)}, f32[32,1024]{1,0:T(8,128)S(1)}, f32[32,1...) fusion(f32[32,8,2048]{2,1,0:T(8,128)S(1)} %copy-done.1, ...), kind=kLoop, calls=%fused_computation.52 | loop fusion | flops 8126464 | bytes 11534336 | tf_op jit(solution)/shard_map/reduce_sum | solution.py:43
  137.7 1.1 pad_maximum_fusion
  138.8 0.0 all-gather.3.cloned.1.call-update
  138.8 4.3 %fusion.24 = (f32[1024,257]{0,1:T(8,128)S(1)}, f32[1024,257]{0,1:T(8,128)S(1)}) fusion(s32[257]{0:T(512)S(1)} %add_select_fusion.2), kind=kLoop, calls=%fused_computation.53 | loop fusion | flops 3947520 | bytes 2106372 | tf_op jit(solution)/shard_map/cos | solution.py:30
  143.2 45.3 %all-gather.3.cloned.1.call-done = f32[64,4,2048]{2,0,1:T(8,128)} async-done(((f32[32,4,2048]{2,0,1:T(8,128)}), f32[64,4,2048]{2,0,1:T(8,128)}) %all-gather.3.cloned.1.call-update) | async-done | bytes 2097168 | tf_op jit(solution)/shard_map/all_gather | solution.py:68
  188.5 2.8 %reduce_sum.99 = f32[32,4,2048]{2,0,1:T(8,128)} reduce(f32[2,32,4,2048]{3,1,0,2:T(8,128)} %bitcast.60, f32[]{:T(128)} %constant.52.clone.1), dimensions={0}, to_apply=%region_9.11 | reduce | flops 262144 | bytes 3145732 | tf_op jit(solution)/shard_map/reduce_sum | solution.py:68
  191.3 4.1 %fusion.16 = f32[32,4,257]{2,0,1:T(8,128)S(1)} fusion(f32[32,4,2048]{2,0,1:T(8,128)} %reduce_sum.99, f32[1024,257]{0,1:T(8,128)S(1)} %get-tuple-element.40, f32[1024,257]{0,1:T(8,128)S(1)} %get-tuple-element.39), kind=kOutput, calls=%fused_computation.31 | convolution fusion | flops 809011328 | bytes 3285504 | tf_op jit(solution)/shard_map/dot_general | solution.py:70
  195.4 0.2 reverse
  195.7 0.1 slice_bitcast_fusion.3
  195.8 10.9 %collective-permute-start.7 = (f32[32,257]{1,0:T(8,128)S(1)}, f32[32,257]{1,0:T(8,128)S(1)}, u32[]{:S(2)}, u32[]{:S(2)}) collective-permute-start(f32[32,257]{1,0:T(8,128)S(1)} %slice_bitcast_fusion.3), channel_id=1, source_target_pairs={{0,504},{2,506},{4,508},{6,510},{8,0},{10,2},{12,4},{14,6},{16,8},... | collective-permute-start | bytes 98696 | tf_op jit(solution)/shard_map/ppermute | solution.py:12
  206.6 0.2 reverse.1
  206.9 0.1 slice_bitcast_fusion.2
  206.9 3.9 %collective-permute-start.6 = (f32[32,257]{1,0:T(8,128)S(1)}, f32[32,257]{1,0:T(8,128)S(1)}, u32[]{:S(2)}, u32[]{:S(2)}) collective-permute-start(f32[32,257]{1,0:T(8,128)S(1)} %slice_bitcast_fusion.2), channel_id=1, source_target_pairs={{0,506},{2,508},{4,510},{6,0},{8,2},{10,4},{12,6},{14,8},{16,10},{... | collective-permute-start | bytes 98696 | tf_op jit(solution)/shard_map/ppermute | solution.py:12
  210.8 0.2 reverse.2
  211.1 0.1 slice_bitcast_fusion.1
  211.2 3.1 %collective-permute-start.5 = (f32[32,257]{1,0:T(8,128)S(1)}, f32[32,257]{1,0:T(8,128)S(1)}, u32[]{:S(2)}, u32[]{:S(2)}) collective-permute-start(f32[32,257]{1,0:T(8,128)S(1)} %slice_bitcast_fusion.1), channel_id=1, source_target_pairs={{0,508},{2,510},{4,0},{6,2},{8,4},{10,6},{12,8},{14,10},{16,12},{1... | collective-permute-start | bytes 98696 | tf_op jit(solution)/shard_map/ppermute | solution.py:12
  214.2 0.2 reverse.3
  214.5 0.1 slice_bitcast_fusion
  214.6 1.9 collective-permute-start.4
  216.5 0.8 copy.9
  217.3 0.0 collective-permute-done.7
  217.3 0.0 collective-permute-done.6
  217.3 0.0 collective-permute-done.5
  217.3 2.7 %collective-permute-done.4 = f32[32,257]{1,0:T(8,128)S(1)} collective-permute-done((f32[32,257]{1,0:T(8,128)S(1)}, f32[32,257]{1,0:T(8,128)S(1)}, u32[]{:S(2)}, u32[]{:S(2)}) %collective-permute-start.4) | collective-permute-done | bytes 32928 | tf_op jit(solution)/shard_map/ppermute | solution.py:12
  220.0 0.8 copy.10
  (14 shorter events, 0.2 us)
Async XLA Ops:
  7.2 33.9 %copy-start = (bf16[32,8,2048]{2,1,0:T(8,128)(2,1)S(1)}, bf16[32,8,2048]{2,1,0:T(8,128)(2,1)}, u32[]{:S(2)}) copy-start(bf16[32,8,2048]{2,1,0:T(8,128)(2,1)} %param.5) | copy-start | bytes 3145732
  7.2 33.9 %copy-start.4 = (s32[32]{0:T(128)S(1)}, s32[32]{0:T(128)}, u32[]{:S(2)}) copy-start(s32[32]{0:T(128)} %param.7) | copy-start | bytes 388
  7.2 181.3 %all-gather.3.cloned.1.call-start = ((), (), s32[]{:S(2)}) async-start(), calls=%async_computation | async-start | bytes 3145728 | tf_op jit(solution)/shard_map/all_gather | solution.py:68
  46.3 39.9 %copy-start.3 = (s32[4,32]{1,0:T(4,128)S(1)}, s32[4,32]{1,0:T(4,128)}, u32[]{:S(2)}) copy-start(s32[4,32]{1,0:T(4,128)} %param.6) | copy-start | bytes 1540
  48.2 16.3 %collective-permute-start = (bf16[32,8,2048]{2,1,0:T(8,128)(2,1)S(1)}, bf16[32,8,2048]{2,1,0:T(8,128)(2,1)S(1)}, u32[]{:S(2)}, u32[]{:S(2)}) collective-permute-start(bf16[32,8,2048]{2,1,0:T(8,128)(2,1)S(1)} %get-tuple-element.28), channel_id=1, source_target_pairs={{0,2},{2,4},{4,6},{6,8},{8,10},{10,12},{12,14},{14,16},{16,18},{18... | collective-permute-start | bytes 3145736 | tf_op jit(solution)/shard_map/ppermute | solution.py:12
  64.6 1.0 copy-start.2
  65.5 17.6 %collective-permute-start.1 = (bf16[32,8,2048]{2,1,0:T(8,128)(2,1)S(1)}, bf16[32,8,2048]{2,1,0:T(8,128)(2,1)}, u32[]{:S(2)}, u32[]{:S(2)}) collective-permute-start(bf16[32,8,2048]{2,1,0:T(8,128)(2,1)S(1)} %collective-permute-done), channel_id=1, source_target_pairs={{0,2},{2,4},{4,6},{6,8},{8,10},{10,12},{12,14},{14,16},{16,18},{18... | collective-permute-start | bytes 3145736 | tf_op jit(solution)/shard_map/ppermute | solution.py:12
  83.1 22.1 %collective-permute-start.2 = (bf16[32,8,2048]{2,1,0:T(8,128)(2,1)}, bf16[32,8,2048]{2,1,0:T(8,128)(2,1)}, u32[]{:S(2)}, u32[]{:S(2)}) collective-permute-start(bf16[32,8,2048]{2,1,0:T(8,128)(2,1)} %collective-permute-done.1), channel_id=1, source_target_pairs={{0,2},{2,4},{4,6},{6,8},{8,10},{10,12},{12,14},{14,16},{16,18},{18... | collective-permute-start | bytes 3145736 | tf_op jit(solution)/shard_map/ppermute | solution.py:12
  105.3 22.1 %collective-permute-start.3 = (bf16[32,8,2048]{2,1,0:T(8,128)(2,1)}, bf16[32,8,2048]{2,1,0:T(8,128)(2,1)}, u32[]{:S(2)}, u32[]{:S(2)}) collective-permute-start(bf16[32,8,2048]{2,1,0:T(8,128)(2,1)} %collective-permute-done.2), channel_id=1, source_target_pairs={{0,2},{2,4},{4,6},{6,8},{8,10},{10,12},{12,14},{14,16},{16,18},{18... | collective-permute-start | bytes 3145736 | tf_op jit(solution)/shard_map/ppermute | solution.py:12
  130.3 1.9 copy-start.1
  195.8 21.5 %collective-permute-start.7 = (f32[32,257]{1,0:T(8,128)S(1)}, f32[32,257]{1,0:T(8,128)S(1)}, u32[]{:S(2)}, u32[]{:S(2)}) collective-permute-start(f32[32,257]{1,0:T(8,128)S(1)} %slice_bitcast_fusion.3), channel_id=1, source_target_pairs={{0,504},{2,506},{4,508},{6,510},{8,0},{10,2},{12,4},{14,6},{16,8},... | collective-permute-start | bytes 98696 | tf_op jit(solution)/shard_map/ppermute | solution.py:12
  206.9 10.4 %collective-permute-start.6 = (f32[32,257]{1,0:T(8,128)S(1)}, f32[32,257]{1,0:T(8,128)S(1)}, u32[]{:S(2)}, u32[]{:S(2)}) collective-permute-start(f32[32,257]{1,0:T(8,128)S(1)} %slice_bitcast_fusion.2), channel_id=1, source_target_pairs={{0,506},{2,508},{4,510},{6,0},{8,2},{10,4},{12,6},{14,8},{16,10},{... | collective-permute-start | bytes 98696 | tf_op jit(solution)/shard_map/ppermute | solution.py:12
  211.2 6.1 %collective-permute-start.5 = (f32[32,257]{1,0:T(8,128)S(1)}, f32[32,257]{1,0:T(8,128)S(1)}, u32[]{:S(2)}, u32[]{:S(2)}) collective-permute-start(f32[32,257]{1,0:T(8,128)S(1)} %slice_bitcast_fusion.1), channel_id=1, source_target_pairs={{0,508},{2,510},{4,0},{6,2},{8,4},{10,6},{12,8},{14,10},{16,12},{1... | collective-permute-start | bytes 98696 | tf_op jit(solution)/shard_map/ppermute | solution.py:12
  214.6 5.4 %collective-permute-start.4 = (f32[32,257]{1,0:T(8,128)S(1)}, f32[32,257]{1,0:T(8,128)S(1)}, u32[]{:S(2)}, u32[]{:S(2)}) collective-permute-start(f32[32,257]{1,0:T(8,128)S(1)} %slice_bitcast_fusion), channel_id=1, source_target_pairs={{0,510},{2,0},{4,2},{6,4},{8,6},{10,8},{12,10},{14,12},{16,14},{18... | collective-permute-start | bytes 98696 | tf_op jit(solution)/shard_map/ppermute | solution.py:12
Sparse Core Ops, SparseCore 0:
  138.9 49.4 all-gather.2
